TPU v7x, 32 devices: a whole 2x2x4 slice. The times are simulated.
32 devices in a mesh: grp: 2 (over y), row: 8 (over z, x), chan: 2 (over core).
Axes of the slice: x: 2, y: 2, z: 4, core: 2. Of those that a mesh axis runs over, the one named last changes fastest.
Arguments:
- band_strip: bfloat16 [424, 64, 128], P('chan', ('grp', 'row')), parts along dimension 1, may hold values from -6 to 6
- conv_weight: bfloat16 [1024, 9, 424], P('row', None, 'chan'), may hold values from -0.09375 to 0.09375
- gdn_gamma: bfloat16 [1024, 1024], P('chan'), as said below
- gdn_beta: float32 [1024], P('chan'), may hold values from 0.5 to 2
- cotangent: bfloat16 [1024, 64, 128], P('chan', ('grp', 'row')), parts along dimension 1, may hold values from -6 to 6
Outputs:
- latent: bfloat16 [1024, 64, 128], P('chan', ('grp', 'row')), parts along dimension 1
- grad_strip: float32 [424, 64, 128], P('chan', ('grp', 'row')), parts along dimension 1
- grad_gamma: float32 [2048, 1024], P(('grp', 'chan')), parts along dimension 0
- grad_beta: float32 [2048], P(('grp', 'chan')), parts along dimension 0
There are 2 independent parts, one for each index of `grp`. A program takes and returns all parts, laid end to end along the dimension named above; an argument that names none is the same for every part. Nothing has to cross between parts.
Inputs may be any that keep to these rules, and one draw needn't show every extreme that they name: `gdn_gamma`: gamma's entries are non-negative.
All inputs are finite; a program needn't handle non-finite values.
Results may differ from a plain program's by a relative error of at most 0.0054.
Values may be sent and summed in bfloat16 or wider, within the bound.
No kernel may reach another device: no remote copies, remote signals or barrier semaphores. Data moves between devices by JAX's collectives and lax.ppermute only.
A program may use at most 64 MiB of HBM per device.

v0:
```python
import math
import jax
import jax.numpy as jnp
from jax import lax
from jax.sharding import PartitionSpec as P

TAPS = ((-1, -1), (-1, 0), (-1, 1), (0, -1), (0, 0), (0, 1), (1, -1), (1, 0), (1, 1))
SWAP = [(0, 1), (1, 0)]


def extended(shard, sides, width):
    for axis, dim in sides:
        count, length = (lax.axis_size(axis), shard.shape[dim])
        up = [(i, (i + 1) % count) for i in range(count - 1)]
        down = [(j, i) for i, j in up]
        last = lax.slice_in_dim(shard, length - width, length, axis=dim)
        leading = lax.slice_in_dim(shard, 0, width, axis=dim)
        before = lax.ppermute(last, axis, up)
        after = lax.ppermute(leading, axis, down)
        shard = jnp.concatenate([before, shard, after], axis=dim)
    return shard


def tap_columns(rimmed, row_count, col_count):
    padded = jnp.pad(rimmed, ((0, 0), (0, 0), (1, 1)))
    stacked = jnp.stack(
        [
            padded[
                :,
                1 + row_shift : 1 + row_shift + row_count,
                1 + col_shift : 1 + col_shift + col_count,
            ]
            for row_shift, col_shift in TAPS
        ],
        axis=0,
    )
    return stacked.reshape(9 * rimmed.shape[0], row_count * col_count)


def chan_gather(x):
    other = lax.ppermute(x, "chan", SWAP)
    first = lax.axis_index("chan") == 0
    return jnp.where(first, jnp.concatenate([x, other], 0), jnp.concatenate([other, x], 0))


def chan_scatter_sum(x):
    half = x.shape[0] // 2
    first = lax.axis_index("chan") == 0
    top, bottom = (x[:half], x[half:])
    mine = jnp.where(first, top, bottom)
    theirs = jnp.where(first, bottom, top)
    return mine + lax.ppermute(theirs, "chan", SWAP)


def ring_order(mesh):
    count = mesh.shape["row"]
    try:
        coords = [tuple(d.coords) for d in mesh.devices[0, :, 0]]
    except Exception:
        return list(range(count))
    xs = sorted({c[0] for c in coords})
    zs = sorted({c[2] for c in coords})
    if len(xs) * len(zs) != count or len(zs) % 2:
        return list(range(count))
    where = {(c[0], c[2]): i for i, c in enumerate(coords)}
    path = [where[xs[0], zs[0]]]
    for k, z in enumerate(zs):
        cols = xs[1:] if k % 2 == 0 else xs[:0:-1]
        path += [where[x, z] for x in cols]
    path += [where[xs[0], z] for z in zs[:0:-1]]
    return path if len(set(path)) == count else list(range(count))


def ring_sum(blocks, ring):
    count = len(ring)
    forward = [(ring[i], ring[(i + 1) % count]) for i in range(count)]
    backward = [(b, a) for a, b in forward]
    position = jnp.asarray([ring.index(i) for i in range(count)], jnp.int32)[lax.axis_index("row")]

    def chunks(x, part):
        half = x.shape[0] // 2
        piece = x[part * half : (part + 1) * half]
        return piece.reshape((count, half // count) + x.shape[1:])

    split = [[chunks(x, part) for x in blocks] for part in range(2)]
    moves = (forward, backward)
    signs = (1, -1)

    def pick(part, step):
        index = (position - signs[part] * (1 + step)) % count
        return [jnp.take(c, index, axis=0) for c in split[part]]

    carry = [pick(part, 0) for part in range(2)]
    for step in range(1, count):
        for part in range(2):
            got = lax.ppermute(carry[part], "row", moves[part])
            carry[part] = [g + o for g, o in zip(got, pick(part, step))]
    gathered = [[c] for c in carry]
    for step in range(1, count):
        for part in range(2):
            gathered[part].append(lax.ppermute(gathered[part][-1], "row", moves[part]))
    results = []
    for leaf in range(len(blocks)):
        halves = []
        for part in range(2):
            stacked = jnp.stack([g[leaf] for g in gathered[part]], 0)
            order = signs[part] * (position - jnp.arange(count)) % count
            halves.append(jnp.take(stacked, order, axis=0).reshape((-1,) + stacked.shape[2:]))
        results.append(jnp.concatenate(halves, 0))
    return results


def make_per_device(ring):

    def per_device(band_strip, conv_weight, gdn_gamma, gdn_beta, cotangent):
        in_local = band_strip.shape[0]
        row_count = band_strip.shape[1]
        col_count = band_strip.shape[2]
        pixels = row_count * col_count
        lat_local = gdn_gamma.shape[0]
        first = lax.axis_index("chan") == 0
        rimmed = extended(band_strip, (("row", 1),), 1)
        columns = tap_columns(rimmed, row_count, col_count)
        shard_piece = lax.all_gather(conv_weight, "row", axis=0, tiled=True)
        flat = shard_piece.reshape(shard_piece.shape[0], 9 * in_local)
        partial_value = jnp.dot(flat, columns, preferred_element_type=jnp.float32)
        pre = chan_scatter_sum(partial_value)
        squares_own = (pre * pre).astype(jnp.bfloat16)
        squares = chan_gather(squares_own)
        norm_value = gdn_beta[:, None] + jnp.dot(
            gdn_gamma, squares, preferred_element_type=jnp.float32
        )
        inverse = lax.rsqrt(norm_value)
        latent = (pre * inverse).astype(jnp.bfloat16)
        upstream = cotangent.reshape(lat_local, pixels).astype(jnp.float32)
        shares = (-0.5 * upstream * pre * inverse * inverse * inverse).astype(jnp.bfloat16)
        gamma_left, gamma_right = (gdn_gamma[:, :lat_local], gdn_gamma[:, lat_local:])
        gamma_mine = jnp.where(first, gamma_left, gamma_right)
        gamma_theirs = lax.ppermute(jnp.where(first, gamma_right, gamma_left), "chan", SWAP)
        gamma_cols = jnp.where(
            first,
            jnp.concatenate([gamma_mine, gamma_theirs], 0),
            jnp.concatenate([gamma_theirs, gamma_mine], 0),
        )
        shares_all = chan_gather(shares)
        back_sum = lax.dot_general(
            gamma_cols, shares_all, (((0,), (0,)), ((), ())), preferred_element_type=jnp.float32
        )
        latent_grad = (upstream * inverse + 2.0 * pre * back_sum).astype(jnp.bfloat16)
        gamma_terms = lax.dot_general(
            shares, squares, (((1,), (1,)), ((), ())), preferred_element_type=jnp.float32
        )
        beta_terms = jnp.sum(shares.astype(jnp.float32), axis=1)
        if len(ring) <= 16:
            gamma_total, beta_total = ring_sum([gamma_terms, beta_terms], ring)
        else:
            gamma_total, beta_total = lax.psum((gamma_terms, beta_terms), "row")
        scale_factor = 1.0 / math.sqrt(pixels * lax.axis_size("row"))
        grad_gamma = gamma_total * scale_factor
        grad_beta = beta_total * scale_factor
        grad_all = chan_gather(latent_grad.reshape(lat_local, row_count, col_count))
        grad_rimmed = extended(grad_all, (("row", 1),), 1)
        grad_padded = jnp.pad(grad_rimmed, ((0, 0), (0, 0), (1, 1)))
        running = jnp.zeros((in_local, pixels), jnp.float32)
        count_rows = shard_piece.shape[0]
        for tap_index, (row_shift, col_shift) in enumerate(TAPS):
            window = grad_padded[
                :,
                1 - row_shift : 1 - row_shift + row_count,
                1 - col_shift : 1 - col_shift + col_count,
            ].reshape(count_rows, pixels)
            running = running + lax.dot_general(
                shard_piece[:, tap_index, :],
                window,
                (((0,), (0,)), ((), ())),
                preferred_element_type=jnp.float32,
            )
        return (
            latent.reshape(lat_local, row_count, col_count),
            running.reshape(in_local, row_count, col_count),
            grad_gamma,
            grad_beta,
        )

    return per_device


def solution(mesh):
    return jax.shard_map(
        make_per_device(ring_order(mesh)),
        mesh=mesh,
        in_specs=(
            P("chan", ("grp", "row"), None),
            P("row", None, "chan"),
            P("chan", None),
            P("chan"),
            P("chan", ("grp", "row"), None),
        ),
        out_specs=(
            P("chan", ("grp", "row"), None),
            P("chan", ("grp", "row"), None),
            P(("grp", "chan"), None),
            P(("grp", "chan")),
        ),
        check_vma=False,
    )
```

profile of v0, /device:TPU:0, one launch (start us, length us, event | category | flops | bytes accessed | tf_op | source)
XLA Modules:
  0.0 275.6 jit_solution(1936061474365692763)
XLA Ops:
  9.1 4.9 %collective-permute-start = (bf16[212,1,128]{2,1,0:T(2,128)(2,1)S(1)}, bf16[212,1,128]{2,1,0:T(2,128)(2,1)S(1)}, u32[]{:S(2)}, u32[]{:S(2)}) collective-permute-start(bf16[212,1,128]{2,1,0:T(2,128)(2,1)S(1)} %get-tuple-element.59), channel_id=1, source_target_pairs={{0,2},{2,4},{4,6},{6,8},{8,10},{10,12},{12,14},{1,3},{3,5},{5,7},{... | collective-permute-start | bytes 162824 | tf_op jit(solution)/shard_map/ppermute | solution.py:18
  16.3 4.3 %collective-permute-done.1 = bf16[212,1,128]{2,1,0:T(2,128)(2,1)S(1)} collective-permute-done((bf16[212,1,128]{2,1,0:T(2,128)(2,1)S(1)}, bf16[212,1,128]{2,1,0:T(2,128)(2,1)S(1)}, u32[]{:S(2)}, u32[]{:S(2)}) %collective-permute-start.1) | collective-permute-done | bytes 54304 | tf_op jit(solution)/shard_map/ppermute | solution.py:19
  20.6 2.1 fusion.40
  27.2 57.8 %all-gather.2.cloned.1.call-done = bf16[1024,9,212]{0,2,1:T(8,128)(2,1)} async-done(((bf16[128,9,212]{0,2,1:T(8,128)(2,1)}), bf16[1024,9,212]{0,2,1:T(8,128)(2,1)}) %all-gather.2.cloned.1.call-update) | async-done | bytes 3907600 | tf_op jit(solution)/shard_map/all_gather | solution.py:124
  85.0 5.6 %reshape.111 = bf16[1024,1908]{0,1:T(8,128)(2,1)} reshape(bf16[1024,9,212]{0,2,1:T(8,128)(2,1)} %all-gather.2.cloned.1.call-done) | data formatting | bytes 7815168 | tf_op jit(solution)/shard_map/reshape | solution.py:125
  90.6 5.1 %convolution_bitcast_fusion = f32[1024,512]{0,1:T(8,128)S(1)} fusion(bf16[1908,512]{1,0:T(8,128)(2,1)} %bitcast.291, bf16[1024,1908]{0,1:T(8,128)(2,1)} %reshape.111), kind=kOutput, calls=%fused_computation.16 | convolution fusion | flops 2000683008 | bytes 7958528 | tf_op jit(solution)/shard_map/dot_general | solution.py:126
  112.1 2.4 copy.10
  121.0 2.2 convert_reduce_fusion
  124.4 2.0 collective-permute-start.37
  126.4 2.1 fusion.62
  175.4 2.2 collective-permute-done.64
  184.2 2.0 collective-permute-start.24
  186.2 2.9 %collective-permute-done.10 = f32[32,1024]{1,0:T(8,128)S(1)} collective-permute-done((f32[32,1024]{1,0:T(8,128)S(1)}, f32[32,1024]{1,0:T(8,128)S(1)}, u32[]{:S(2)}, u32[]{:S(2)}) %collective-permute-start.10) | collective-permute-done | bytes 131104 | tf_op jit(solution)/shard_map/ppermute | solution.py:96
  189.2 2.0 collective-permute-start.25
  191.2 2.9 %collective-permute-done.11 = f32[32,1024]{1,0:T(8,128)S(1)} collective-permute-done((f32[32,1024]{1,0:T(8,128)S(1)}, f32[32,1024]{1,0:T(8,128)S(1)}, u32[]{:S(2)}, u32[]{:S(2)}) %collective-permute-start.11) | collective-permute-done | bytes 131104 | tf_op jit(solution)/shard_map/ppermute | solution.py:96
  194.3 2.0 collective-permute-start.26
  196.2 2.9 %collective-permute-done.12 = f32[32,1024]{1,0:T(8,128)S(1)} collective-permute-done((f32[32,1024]{1,0:T(8,128)S(1)}, f32[32,1024]{1,0:T(8,128)S(1)}, u32[]{:S(2)}, u32[]{:S(2)}) %collective-permute-start.12) | collective-permute-done | bytes 131104 | tf_op jit(solution)/shard_map/ppermute | solution.py:96
  199.3 2.0 collective-permute-start.27
  201.3 2.7 fusion.32
  204.3 2.0 collective-permute-start.28
  206.3 3.8 %collective-permute-done.14 = f32[32,1024]{1,0:T(8,128)S(1)} collective-permute-done((f32[32,1024]{1,0:T(8,128)S(1)}, f32[32,1024]{1,0:T(8,128)S(1)}, u32[]{:S(2)}, u32[]{:S(2)}) %collective-permute-start.14) | collective-permute-done | bytes 131104 | tf_op jit(solution)/shard_map/ppermute | solution.py:96
  212.3 2.9 %collective-permute-done.15 = f32[32,1024]{1,0:T(8,128)S(1)} collective-permute-done((f32[32,1024]{1,0:T(8,128)S(1)}, f32[32,1024]{1,0:T(8,128)S(1)}, u32[]{:S(2)}, u32[]{:S(2)}) %collective-permute-start.15) | collective-permute-done | bytes 131104 | tf_op jit(solution)/shard_map/ppermute | solution.py:96
  217.8 2.4 collective-permute-start.7
  221.5 2.7 collective-permute-start.17
  225.8 6.9 %collective-permute-done.17 = f32[32,1024]{1,0:T(8,128)S(1)} collective-permute-done((f32[32,1024]{1,0:T(8,128)S(1)}, f32[32,1024]{1,0:T(8,128)S(1)}, u32[]{:S(2)}, u32[]{:S(2)}) %collective-permute-start.17) | collective-permute-done | bytes 131104 | tf_op jit(solution)/shard_map/ppermute | solution.py:101
  232.7 2.5 collective-permute-start.18
  242.1 2.0 collective-permute-start.19
  244.3 3.5 %collective-permute-done.19 = f32[32,1024]{1,0:T(8,128)S(1)} collective-permute-done((f32[32,1024]{1,0:T(8,128)S(1)}, f32[32,1024]{1,0:T(8,128)S(1)}, u32[]{:S(2)}, u32[]{:S(2)}) %collective-permute-start.19) | collective-permute-done | bytes 131104 | tf_op jit(solution)/shard_map/ppermute | solution.py:101
  247.8 2.5 collective-permute-start.20
  250.6 3.4 %collective-permute-done.20 = f32[32,1024]{1,0:T(8,128)S(1)} collective-permute-done((f32[32,1024]{1,0:T(8,128)S(1)}, f32[32,1024]{1,0:T(8,128)S(1)}, u32[]{:S(2)}, u32[]{:S(2)}) %collective-permute-start.20) | collective-permute-done | bytes 131104 | tf_op jit(solution)/shard_map/ppermute | solution.py:101
  256.4 3.1 %collective-permute-done.21 = f32[32,1024]{1,0:T(8,128)S(1)} collective-permute-done((f32[32,1024]{1,0:T(8,128)S(1)}, f32[32,1024]{1,0:T(8,128)S(1)}, u32[]{:S(2)}, u32[]{:S(2)}) %collective-permute-start.21) | collective-permute-done | bytes 131104 | tf_op jit(solution)/shard_map/ppermute | solution.py:101
  261.6 2.8 %collective-permute-done.22 = f32[32,1024]{1,0:T(8,128)S(1)} collective-permute-done((f32[32,1024]{1,0:T(8,128)S(1)}, f32[32,1024]{1,0:T(8,128)S(1)}, u32[]{:S(2)}, u32[]{:S(2)}) %collective-permute-start.22) | collective-permute-done | bytes 131104 | tf_op jit(solution)/shard_map/ppermute | solution.py:101
  (269 shorter events, 99.9 us)
Async XLA Ops:
  7.2 77.8 %all-gather.2.cloned.1.call-start = ((), (), s32[]{:S(2)}) async-start(), calls=%async_computation | async-start | bytes 4478976 | tf_op jit(solution)/shard_map/all_gather | solution.py:124
  9.1 7.2 %collective-permute-start = (bf16[212,1,128]{2,1,0:T(2,128)(2,1)S(1)}, bf16[212,1,128]{2,1,0:T(2,128)(2,1)S(1)}, u32[]{:S(2)}, u32[]{:S(2)}) collective-permute-start(bf16[212,1,128]{2,1,0:T(2,128)(2,1)S(1)} %get-tuple-element.59), channel_id=1, source_target_pairs={{0,2},{2,4},{4,6},{6,8},{8,10},{10,12},{12,14},{1,3},{3,5},{5,7},{... | collective-permute-start | bytes 162824 | tf_op jit(solution)/shard_map/ppermute | solution.py:18
  14.0 6.6 %collective-permute-start.1 = (bf16[212,1,128]{2,1,0:T(2,128)(2,1)S(1)}, bf16[212,1,128]{2,1,0:T(2,128)(2,1)S(1)}, u32[]{:S(2)}, u32[]{:S(2)}) collective-permute-start(bf16[212,1,128]{2,1,0:T(2,128)(2,1)S(1)} %get-tuple-element.60), channel_id=1, source_target_pairs={{2,0},{4,2},{6,4},{8,6},{10,8},{12,10},{14,12},{3,1},{5,3},{7,5},{... | collective-permute-start | bytes 162824 | tf_op jit(solution)/shard_map/ppermute | solution.py:19
  96.8 18.9 %collective-permute-start.2 = (f32[512,512]{0,1:T(8,128)}, f32[512,512]{0,1:T(8,128)}, u32[]{:S(2)}, u32[]{:S(2)}) collective-permute-start(f32[512,512]{0,1:T(8,128)} %slice_select_fusion), channel_id=1, source_target_pairs={{0,1},{1,0},{2,3},{3,2},{4,5},{5,4},{6,7},{7,6},{8,9},{9,8},{10,11... | collective-permute-start | bytes 3145736 | tf_op jit(solution)/shard_map/ppermute | solution.py:52
  100.5 100.8 %collective-permute-start.4 = (bf16[512,512]{0,1:T(8,128)(2,1)}, bf16[512,512]{0,1:T(8,128)(2,1)}, u32[]{:S(2)}, u32[]{:S(2)}) collective-permute-start(bf16[512,512]{0,1:T(8,128)(2,1)} %get-tuple-element.56), channel_id=1, source_target_pairs={{0,1},{1,0},{2,3},{3,2},{4,5},{5,4},{6,7},{7,6},{8,9},{9,8},{10,11... | collective-permute-start | bytes 1572872 | tf_op jit(solution)/shard_map/ppermute | solution.py:139
  124.4 6.6 %collective-permute-start.51 = (f32[32]{0:T(128)S(1)}, f32[32]{0:T(128)S(1)}, u32[]{:S(2)}, u32[]{:S(2)}) collective-permute-start(f32[32]{0:T(128)S(1)} %fusion.78), channel_id=1, source_target_pairs={{2,0},{6,2},{10,6},{14,10},{12,14},{8,12},{4,8},{0,4},{3,1},{7,3},... | collective-permute-start | bytes 392 | tf_op jit(solution)/shard_map/ppermute | solution.py:96
  124.4 7.2 %collective-permute-start.37 = (f32[32]{0:T(128)S(1)}, f32[32]{0:T(128)S(1)}, u32[]{:S(2)}, u32[]{:S(2)}) collective-permute-start(f32[32]{0:T(128)S(1)} %fusion.63), channel_id=1, source_target_pairs={{0,2},{2,6},{6,10},{10,14},{14,12},{12,8},{8,4},{4,0},{1,3},{3,7},... | collective-permute-start | bytes 392 | tf_op jit(solution)/shard_map/ppermute | solution.py:96
  126.4 74.8 %collective-permute-start.5 = (bf16[512,512]{0,1:T(8,128)(2,1)}, bf16[512,512]{0,1:T(8,128)(2,1)}, u32[]{:S(2)}, u32[]{:S(2)}) collective-permute-start(bf16[512,512]{0,1:T(8,128)(2,1)} %get-tuple-element.35), channel_id=1, source_target_pairs={{0,1},{1,0},{2,3},{3,2},{4,5},{5,4},{6,7},{7,6},{8,9},{9,8},{10,11... | collective-permute-start | bytes 1572872 | tf_op jit(solution)/shard_map/ppermute | solution.py:41
  129.5 54.5 %collective-permute-start.9 = (f32[32,1024]{1,0:T(8,128)}, f32[32,1024]{1,0:T(8,128)S(1)}, u32[]{:S(2)}, u32[]{:S(2)}) collective-permute-start(f32[32,1024]{1,0:T(8,128)} %select_bitcast_fusion.1), channel_id=1, source_target_pairs={{0,2},{2,6},{6,10},{10,14},{14,12},{12,8},{8,4},{4,0},{1,3},{3,7},... | collective-permute-start | bytes 393224 | tf_op jit(solution)/shard_map/ppermute | solution.py:96
  175.1 9.1 %collective-permute-start.23 = (f32[32,1024]{1,0:T(8,128)S(1)}, f32[32,1024]{1,0:T(8,128)S(1)}, u32[]{:S(2)}, u32[]{:S(2)}) collective-permute-start(f32[32,1024]{1,0:T(8,128)S(1)} %select_bitcast_fusion), channel_id=1, source_target_pairs={{2,0},{6,2},{10,6},{14,10},{12,14},{8,12},{4,8},{0,4},{3,1},{7,3},... | collective-permute-start | bytes 393224 | tf_op jit(solution)/shard_map/ppermute | solution.py:96
  184.0 5.0 %collective-permute-start.10 = (f32[32,1024]{1,0:T(8,128)S(1)}, f32[32,1024]{1,0:T(8,128)S(1)}, u32[]{:S(2)}, u32[]{:S(2)}) collective-permute-start(f32[32,1024]{1,0:T(8,128)S(1)} %bitcast_add_fusion.13), channel_id=1, source_target_pairs={{0,2},{2,6},{6,10},{10,14},{14,12},{12,8},{8,4},{4,0},{1,3},{3,7},... | collective-permute-start | bytes 393224 | tf_op jit(solution)/shard_map/ppermute | solution.py:96
  184.2 5.0 %collective-permute-start.24 = (f32[32,1024]{1,0:T(8,128)S(1)}, f32[32,1024]{1,0:T(8,128)S(1)}, u32[]{:S(2)}, u32[]{:S(2)}) collective-permute-start(f32[32,1024]{1,0:T(8,128)S(1)} %bitcast_add_fusion.6), channel_id=1, source_target_pairs={{2,0},{6,2},{10,6},{14,10},{12,14},{8,12},{4,8},{0,4},{3,1},{7,3},... | collective-permute-start | bytes 393224 | tf_op jit(solution)/shard_map/ppermute | solution.py:96
  189.0 5.0 %collective-permute-start.11 = (f32[32,1024]{1,0:T(8,128)S(1)}, f32[32,1024]{1,0:T(8,128)S(1)}, u32[]{:S(2)}, u32[]{:S(2)}) collective-permute-start(f32[32,1024]{1,0:T(8,128)S(1)} %bitcast_add_fusion.12), channel_id=1, source_target_pairs={{0,2},{2,6},{6,10},{10,14},{14,12},{12,8},{8,4},{4,0},{1,3},{3,7},... | collective-permute-start | bytes 393224 | tf_op jit(solution)/shard_map/ppermute | solution.py:96
  199.3 5.0 %collective-permute-start.27 = (f32[32,1024]{1,0:T(8,128)S(1)}, f32[32,1024]{1,0:T(8,128)S(1)}, u32[]{:S(2)}, u32[]{:S(2)}) collective-permute-start(f32[32,1024]{1,0:T(8,128)S(1)} %bitcast_add_fusion.3), channel_id=1, source_target_pairs={{2,0},{6,2},{10,6},{14,10},{12,14},{8,12},{4,8},{0,4},{3,1},{7,3},... | collective-permute-start | bytes 393224 | tf_op jit(solution)/shard_map/ppermute | solution.py:96
  204.1 13.3 %collective-permute-start.6 = (bf16[512,4,128]{0,2,1:T(8,128)(2,1)S(1)}, bf16[512,4,128]{0,2,1:T(8,128)(2,1)S(1)}, u32[]{:S(2)}, u32[]{:S(2)}) collective-permute-start(bf16[512,4,128]{0,2,1:T(8,128)(2,1)S(1)} %bitcast.292), channel_id=1, source_target_pairs={{0,1},{1,0},{2,3},{3,2},{4,5},{5,4},{6,7},{7,6},{8,9},{9,8},{10,11... | collective-permute-start | bytes 1572872 | tf_op jit(solution)/shard_map/ppermute | solution.py:41
  204.2 5.9 %collective-permute-start.14 = (f32[32,1024]{1,0:T(8,128)S(1)}, f32[32,1024]{1,0:T(8,128)S(1)}, u32[]{:S(2)}, u32[]{:S(2)}) collective-permute-start(f32[32,1024]{1,0:T(8,128)S(1)} %bitcast_add_fusion.9), channel_id=1, source_target_pairs={{0,2},{2,6},{6,10},{10,14},{14,12},{12,8},{8,4},{4,0},{1,3},{3,7},... | collective-permute-start | bytes 393224 | tf_op jit(solution)/shard_map/ppermute | solution.py:96
  204.3 6.1 %collective-permute-start.28 = (f32[32,1024]{1,0:T(8,128)S(1)}, f32[32,1024]{1,0:T(8,128)S(1)}, u32[]{:S(2)}, u32[]{:S(2)}) collective-permute-start(f32[32,1024]{1,0:T(8,128)S(1)} %bitcast_add_fusion.2), channel_id=1, source_target_pairs={{2,0},{6,2},{10,6},{14,10},{12,14},{8,12},{4,8},{0,4},{3,1},{7,3},... | collective-permute-start | bytes 393224 | tf_op jit(solution)/shard_map/ppermute | solution.py:96
  210.1 5.1 %collective-permute-start.15 = (f32[32,1024]{1,0:T(8,128)S(1)}, f32[32,1024]{1,0:T(8,128)S(1)}, u32[]{:S(2)}, u32[]{:S(2)}) collective-permute-start(f32[32,1024]{1,0:T(8,128)S(1)} %bitcast_add_fusion.8), channel_id=1, source_target_pairs={{0,2},{2,6},{6,10},{10,14},{14,12},{12,8},{8,4},{4,0},{1,3},{3,7},... | collective-permute-start | bytes 393224 | tf_op jit(solution)/shard_map/ppermute | solution.py:96
  210.5 5.3 %collective-permute-start.29 = (f32[32,1024]{1,0:T(8,128)S(1)}, f32[32,1024]{1,0:T(8,128)S(1)}, u32[]{:S(2)}, u32[]{:S(2)}) collective-permute-start(f32[32,1024]{1,0:T(8,128)S(1)} %bitcast_add_fusion.1), channel_id=1, source_target_pairs={{2,0},{6,2},{10,6},{14,10},{12,14},{8,12},{4,8},{0,4},{3,1},{7,3},... | collective-permute-start | bytes 393224 | tf_op jit(solution)/shard_map/ppermute | solution.py:96
  215.2 6.2 %collective-permute-start.16 = (f32[32,1024]{1,0:T(8,128)S(1)}, f32[32,1024]{1,0:T(8,128)S(1)}, u32[]{:S(2)}, u32[]{:S(2)}) collective-permute-start(f32[32,1024]{1,0:T(8,128)S(1)} %get-tuple-element.37), channel_id=1, source_target_pairs={{0,2},{2,6},{6,10},{10,14},{14,12},{12,8},{8,4},{4,0},{1,3},{3,7},... | collective-permute-start | bytes 393224 | tf_op jit(solution)/shard_map/ppermute | solution.py:101
  215.8 8.4 %collective-permute-start.30 = (f32[32,1024]{1,0:T(8,128)S(1)}, f32[32,1024]{1,0:T(8,128)S(1)}, u32[]{:S(2)}, u32[]{:S(2)}) collective-permute-start(f32[32,1024]{1,0:T(8,128)S(1)} %get-tuple-element.39), channel_id=1, source_target_pairs={{2,0},{6,2},{10,6},{14,10},{12,14},{8,12},{4,8},{0,4},{3,1},{7,3},... | collective-permute-start | bytes 393224 | tf_op jit(solution)/shard_map/ppermute | solution.py:101
  217.8 17.5 %collective-permute-start.7 = (bf16[1024,1,128]{0,2,1:T(8,128)(2,1)S(1)}, bf16[1024,1,128]{0,2,1:T(8,128)(2,1)S(1)}, u32[]{:S(2)}, u32[]{:S(2)}) collective-permute-start(bf16[1024,1,128]{0,2,1:T(8,128)(2,1)S(1)} %get-tuple-element.53), channel_id=1, source_target_pairs={{0,2},{2,4},{4,6},{6,8},{8,10},{10,12},{12,14},{1,3},{3,5},{5,7},{... | collective-permute-start | bytes 786440 | tf_op jit(solution)/shard_map/ppermute | solution.py:18
  220.2 15.1 %collective-permute-start.8 = (bf16[1024,1,128]{0,2,1:T(8,128)(2,1)S(1)}, bf16[1024,1,128]{0,2,1:T(8,128)(2,1)S(1)}, u32[]{:S(2)}, u32[]{:S(2)}) collective-permute-start(bf16[1024,1,128]{0,2,1:T(8,128)(2,1)S(1)} %get-tuple-element.54), channel_id=1, source_target_pairs={{2,0},{4,2},{6,4},{8,6},{10,8},{12,10},{14,12},{3,1},{5,3},{7,5},{... | collective-permute-start | bytes 786440 | tf_op jit(solution)/shard_map/ppermute | solution.py:19
  221.5 11.2 %collective-permute-start.17 = (f32[32,1024]{1,0:T(8,128)S(1)}, f32[32,1024]{1,0:T(8,128)S(1)}, u32[]{:S(2)}, u32[]{:S(2)}) collective-permute-start(f32[32,1024]{1,0:T(8,128)S(1)} %collective-permute-done.16), channel_id=1, source_target_pairs={{0,2},{2,6},{6,10},{10,14},{14,12},{12,8},{8,4},{4,0},{1,3},{3,7},... | collective-permute-start | bytes 393224 | tf_op jit(solution)/shard_map/ppermute | solution.py:101
  224.2 11.0 %collective-permute-start.31 = (f32[32,1024]{1,0:T(8,128)S(1)}, f32[32,1024]{1,0:T(8,128)S(1)}, u32[]{:S(2)}, u32[]{:S(2)}) collective-permute-start(f32[32,1024]{1,0:T(8,128)S(1)} %collective-permute-done.30), channel_id=1, source_target_pairs={{2,0},{6,2},{10,6},{14,10},{12,14},{8,12},{4,8},{0,4},{3,1},{7,3},... | collective-permute-start | bytes 393224 | tf_op jit(solution)/shard_map/ppermute | solution.py:101
  232.7 9.4 %collective-permute-start.18 = (f32[32,1024]{1,0:T(8,128)S(1)}, f32[32,1024]{1,0:T(8,128)S(1)}, u32[]{:S(2)}, u32[]{:S(2)}) collective-permute-start(f32[32,1024]{1,0:T(8,128)S(1)} %collective-permute-done.17), channel_id=1, source_target_pairs={{0,2},{2,6},{6,10},{10,14},{14,12},{12,8},{8,4},{4,0},{1,3},{3,7},... | collective-permute-start | bytes 393224 | tf_op jit(solution)/shard_map/ppermute | solution.py:101
  235.2 9.0 %collective-permute-start.32 = (f32[32,1024]{1,0:T(8,128)S(1)}, f32[32,1024]{1,0:T(8,128)S(1)}, u32[]{:S(2)}, u32[]{:S(2)}) collective-permute-start(f32[32,1024]{1,0:T(8,128)S(1)} %collective-permute-done.31), channel_id=1, source_target_pairs={{2,0},{6,2},{10,6},{14,10},{12,14},{8,12},{4,8},{0,4},{3,1},{7,3},... | collective-permute-start | bytes 393224 | tf_op jit(solution)/shard_map/ppermute | solution.py:101
  242.1 5.6 %collective-permute-start.19 = (f32[32,1024]{1,0:T(8,128)S(1)}, f32[32,1024]{1,0:T(8,128)S(1)}, u32[]{:S(2)}, u32[]{:S(2)}) collective-permute-start(f32[32,1024]{1,0:T(8,128)S(1)} %collective-permute-done.18), channel_id=1, source_target_pairs={{0,2},{2,6},{6,10},{10,14},{14,12},{12,8},{8,4},{4,0},{1,3},{3,7},... | collective-permute-start | bytes 393224 | tf_op jit(solution)/shard_map/ppermute | solution.py:101
  244.2 6.4 %collective-permute-start.33 = (f32[32,1024]{1,0:T(8,128)S(1)}, f32[32,1024]{1,0:T(8,128)S(1)}, u32[]{:S(2)}, u32[]{:S(2)}) collective-permute-start(f32[32,1024]{1,0:T(8,128)S(1)} %collective-permute-done.32), channel_id=1, source_target_pairs={{2,0},{6,2},{10,6},{14,10},{12,14},{8,12},{4,8},{0,4},{3,1},{7,3},... | collective-permute-start | bytes 393224 | tf_op jit(solution)/shard_map/ppermute | solution.py:101
  247.8 6.3 %collective-permute-start.20 = (f32[32,1024]{1,0:T(8,128)S(1)}, f32[32,1024]{1,0:T(8,128)S(1)}, u32[]{:S(2)}, u32[]{:S(2)}) collective-permute-start(f32[32,1024]{1,0:T(8,128)S(1)} %collective-permute-done.19), channel_id=1, source_target_pairs={{0,2},{2,6},{6,10},{10,14},{14,12},{12,8},{8,4},{4,0},{1,3},{3,7},... | collective-permute-start | bytes 393224 | tf_op jit(solution)/shard_map/ppermute | solution.py:101
  250.6 5.5 %collective-permute-start.34 = (f32[32,1024]{1,0:T(8,128)S(1)}, f32[32,1024]{1,0:T(8,128)S(1)}, u32[]{:S(2)}, u32[]{:S(2)}) collective-permute-start(f32[32,1024]{1,0:T(8,128)S(1)} %collective-permute-done.33), channel_id=1, source_target_pairs={{2,0},{6,2},{10,6},{14,10},{12,14},{8,12},{4,8},{0,4},{3,1},{7,3},... | collective-permute-start | bytes 393224 | tf_op jit(solution)/shard_map/ppermute | solution.py:101
  254.0 5.4 %collective-permute-start.21 = (f32[32,1024]{1,0:T(8,128)S(1)}, f32[32,1024]{1,0:T(8,128)S(1)}, u32[]{:S(2)}, u32[]{:S(2)}) collective-permute-start(f32[32,1024]{1,0:T(8,128)S(1)} %collective-permute-done.20), channel_id=1, source_target_pairs={{0,2},{2,6},{6,10},{10,14},{14,12},{12,8},{8,4},{4,0},{1,3},{3,7},... | collective-permute-start | bytes 393224 | tf_op jit(solution)/shard_map/ppermute | solution.py:101
  (62 other events, 418.4 us)
Sparse Core Ops, SparseCore 0:
  10.0 74.9 all-gather.1
where the time goes:
time: 276 us
  waiting for transfers between devices  122 us (44%)
  starting transfers between devices  69.1 us (25%)
  between operations  25.5 us (9%)
  local copies, waits for them, and re-layouts  24.9 us (9%)
  other arithmetic  17.1 us (6%)
  matrix products  16.6 us (6%)
    all_gather x1, waiting for transfers between devices, per_device(): shard_piece = lax.all_gather(conv_weight, 'row', axis=0, tiled=True)  57.8 us
    ppermute x28, waiting for transfers between devices, ring_sum(): gathered[part].append(lax.ppermute(gathered[part][-1], 'row', moves[part]))  33.7 us
    ppermute x28, starting transfers between devices, ring_sum(): gathered[part].append(lax.ppermute(gathered[part][-1], 'row', moves[part]))  29.6 us
    ppermute x28, starting transfers between devices, ring_sum(): got = lax.ppermute(carry[part], 'row', moves[part])  28.9 us
    ppermute x28, waiting for transfers between devices, ring_sum(): got = lax.ppermute(carry[part], 'row', moves[part])  25 us
    ppermute x2, starting transfers between devices, extended(): before = lax.ppermute(last, axis, up)  7.28 us
    unnamed x79, local copies, waits for them, and re-layouts  7.24 us
    reshape x1, local copies, waits for them, and re-layouts, per_device(): flat = shard_piece.reshape(shard_piece.shape[0], 9 * in_local)  5.57 us
  transfers between devices with their start and end apart: 66, of which 43 were waited for; matrix products, arithmetic and copies ran while one was open for 16% of the time, Pallas kernels for 0%

commit v1 on v0

--- a/solution.py
+++ b/solution.py
@@ -6,6 +6,19 @@
 
 TAPS = ((-1, -1), (-1, 0), (-1, 1), (0, -1), (0, 0), (0, 1), (1, -1), (1, 0), (1, 1))
 SWAP = [(0, 1), (1, 0)]
+
+
+def collect(x, axis, dim):
+    ways = lax.axis_size(axis)
+    up = [(d, (d + 1) % ways) for d in range(ways)]
+    down = [(d, (d - 1) % ways) for d in range(ways)]
+    earlier, later = ([x], [x])
+    for _ in range(ways // 2):
+        earlier.append(lax.ppermute(earlier[-1], axis, up))
+    for _ in range((ways - 1) // 2):
+        later.append(lax.ppermute(later[-1], axis, down))
+    line = jnp.concatenate([*earlier[::-1], *later[1:]], axis=dim)
+    return jnp.roll(line, (lax.axis_index(axis) - ways // 2) * x.shape[dim], axis=dim)
 
 
 def extended(shard, sides, width):
@@ -121,7 +134,7 @@
         first = lax.axis_index("chan") == 0
         rimmed = extended(band_strip, (("row", 1),), 1)
         columns = tap_columns(rimmed, row_count, col_count)
-        shard_piece = lax.all_gather(conv_weight, "row", axis=0, tiled=True)
+        shard_piece = collect(conv_weight, "row", 0)
         flat = shard_piece.reshape(shard_piece.shape[0], 9 * in_local)
         partial_value = jnp.dot(flat, columns, preferred_element_type=jnp.float32)
         pre = chan_scatter_sum(partial_value)

time: 276 us -> 287 us (1.040)
  starting transfers between devices: 69.1 us -> 98 us
  between operations: 25.5 us -> 12.3 us
  waiting for transfers between devices: 122 us -> 109 us
  local copies, waits for them, and re-layouts: 24.9 us -> 33.5 us
    all_gather x1 -> x0, waiting for transfers between devices: 57.8 us -> none  [per_device(): shard_piece = lax.all_gather(conv_weight, 'row', axis=0, tiled=True)]
    ppermute x0 -> x7, waiting for transfers between devices: none -> 35.9 us  [the longest x4 26.3 us: collect(): earlier.append(lax.ppermute(earlier[-1], axis, up))]
    ppermute x0 -> x7, starting transfers between devices: none -> 24.1 us  [the longest x3 16.1 us: collect(): later.append(lax.ppermute(later[-1], axis, down))]
    ppermute x2, waiting for transfers between devices: 0.98 us -> 9.12 us  [extended(): before = lax.ppermute(last, axis, up)]
    unnamed x79 -> x102, local copies, waits for them, and re-layouts: 7.24 us -> 13.2 us
    ppermute x28, waiting for transfers between devices: 33.7 us -> 30.1 us  [ring_sum(): gathered[part].append(lax.ppermute(gathered[part][-1], 'row', moves[part]))]
    ppermute x2, waiting for transfers between devices: 4.34 us -> 7.46 us  [extended(): after = lax.ppermute(leading, axis, down)]
  transfers between devices with their start and end apart: 66 -> 72, of which waited for: 43 -> 49; matrix products, arithmetic and copies ran while one was open for 16% -> 15% of each run, Pallas kernels for 0% -> 0%
where the time goes in v1:
time: 287 us; the launch traced here: 286 us
  waiting for transfers between devices  109 us (38%)
  starting transfers between devices  98 us (34%)
  local copies, waits for them, and re-layouts  33.5 us (12%)
  matrix products  17.2 us (6%)
  other arithmetic  16.4 us (6%)
  between operations  12.3 us (4%)
    ppermute x28, starting transfers between devices, ring_sum(): gathered[part].append(lax.ppermute(gathered[part][-1], 'row', moves[part]))  31.9 us
    ppermute x28, waiting for transfers between devices, ring_sum(): gathered[part].append(lax.ppermute(gathered[part][-1], 'row', moves[part]))  30.1 us
    ppermute x28, starting transfers between devices, ring_sum(): got = lax.ppermute(carry[part], 'row', moves[part])  29.3 us
    ppermute x28, waiting for transfers between devices, ring_sum(): got = lax.ppermute(carry[part], 'row', moves[part])  26.4 us
    ppermute x4, waiting for transfers between devices, collect(): earlier.append(lax.ppermute(earlier[-1], axis, up))  26.3 us
    ppermute x3, starting transfers between devices, collect(): later.append(lax.ppermute(later[-1], axis, down))  16.1 us
    unnamed x102, local copies, waits for them, and re-layouts  13.2 us
    ppermute x3, waiting for transfers between devices, collect(): later.append(lax.ppermute(later[-1], axis, down))  9.58 us
  transfers between devices with their start and end apart: 72, of which 49 were waited for; matrix products, arithmetic and copies ran while one was open for 15% of the time, Pallas kernels for 0%

profile of v1, /device:TPU:0, one launch (start us, length us, event | category | flops | bytes accessed | tf_op | source)
XLA Modules:
  0.0 286.3 jit_solution(2704817336809289584)
XLA Ops:
  0.6 3.0 %collective-permute-start = (bf16[128,9,212]{0,2,1:T(8,128)(2,1)}, bf16[128,9,212]{0,2,1:T(8,128)(2,1)S(1)}, u32[]{:S(2)}, u32[]{:S(2)}) collective-permute-start(bf16[128,9,212]{0,2,1:T(8,128)(2,1)} %param.15), channel_id=1, source_target_pairs={{0,2},{2,4},{4,6},{6,8},{8,10},{10,12},{12,14},{14,0},{1,3},{3,5},... | collective-permute-start | bytes 1465352 | tf_op jit(solution)/shard_map/ppermute | solution.py:17
  6.2 4.6 %collective-permute-start.7 = (bf16[212,1,128]{2,1,0:T(2,128)(2,1)S(1)}, bf16[212,1,128]{2,1,0:T(2,128)(2,1)S(1)}, u32[]{:S(2)}, u32[]{:S(2)}) collective-permute-start(bf16[212,1,128]{2,1,0:T(2,128)(2,1)S(1)} %get-tuple-element.59), channel_id=1, source_target_pairs={{0,2},{2,4},{4,6},{6,8},{8,10},{10,12},{12,14},{1,3},{3,5},{5,7},{... | collective-permute-start | bytes 162824 | tf_op jit(solution)/shard_map/ppermute | solution.py:31
  10.8 2.5 collective-permute-start.4
  13.2 7.5 %collective-permute-done.8 = bf16[212,1,128]{2,1,0:T(2,128)(2,1)S(1)} collective-permute-done((bf16[212,1,128]{2,1,0:T(2,128)(2,1)S(1)}, bf16[212,1,128]{2,1,0:T(2,128)(2,1)S(1)}, u32[]{:S(2)}, u32[]{:S(2)}) %collective-permute-start.8) | collective-permute-done | bytes 54304 | tf_op jit(solution)/shard_map/ppermute | solution.py:32
  20.7 9.1 %collective-permute-done.7 = bf16[212,1,128]{2,1,0:T(2,128)(2,1)S(1)} collective-permute-done((bf16[212,1,128]{2,1,0:T(2,128)(2,1)S(1)}, bf16[212,1,128]{2,1,0:T(2,128)(2,1)S(1)}, u32[]{:S(2)}, u32[]{:S(2)}) %collective-permute-start.7) | collective-permute-done | bytes 54304 | tf_op jit(solution)/shard_map/ppermute | solution.py:31
  31.9 2.5 collective-permute-start.1
  35.0 11.9 %collective-permute-done.1 = bf16[128,9,212]{0,2,1:T(8,128)(2,1)S(1)} collective-permute-done((bf16[128,9,212]{0,2,1:T(8,128)(2,1)S(1)}, bf16[128,9,212]{0,2,1:T(8,128)(2,1)S(1)}, u32[]{:S(2)}, u32[]{:S(2)}) %collective-permute-start.1) | collective-permute-done | bytes 488480 | tf_op jit(solution)/shard_map/ppermute | solution.py:17
  47.5 4.8 %collective-permute-start.5 = (bf16[128,9,212]{0,2,1:T(8,128)(2,1)S(1)}, bf16[128,9,212]{0,2,1:T(8,128)(2,1)S(1)}, u32[]{:S(2)}, u32[]{:S(2)}) collective-permute-start(bf16[128,9,212]{0,2,1:T(8,128)(2,1)S(1)} %collective-permute-done.4), channel_id=1, source_target_pairs={{0,14},{2,0},{4,2},{6,4},{8,6},{10,8},{12,10},{14,12},{1,15},{3,1}... | collective-permute-start | bytes 1465352 | tf_op jit(solution)/shard_map/ppermute | solution.py:19
  52.2 14.5 %collective-permute-done.2 = bf16[128,9,212]{0,2,1:T(8,128)(2,1)S(1)} collective-permute-done((bf16[128,9,212]{0,2,1:T(8,128)(2,1)S(1)}, bf16[128,9,212]{0,2,1:T(8,128)(2,1)S(1)}, u32[]{:S(2)}, u32[]{:S(2)}) %collective-permute-start.2) | collective-permute-done | bytes 488480 | tf_op jit(solution)/shard_map/ppermute | solution.py:17
  66.7 2.5 collective-permute-start.3
  72.4 8.8 %collective-permute-start.6 = (bf16[128,9,212]{0,2,1:T(8,128)(2,1)S(1)}, bf16[128,9,212]{0,2,1:T(8,128)(2,1)S(1)}, u32[]{:S(2)}, u32[]{:S(2)}) collective-permute-start(bf16[128,9,212]{0,2,1:T(8,128)(2,1)S(1)} %collective-permute-done.5), channel_id=1, source_target_pairs={{0,14},{2,0},{4,2},{6,4},{8,6},{10,8},{12,10},{14,12},{1,15},{3,1}... | collective-permute-start | bytes 1465352 | tf_op jit(solution)/shard_map/ppermute | solution.py:19
  82.5 9.6 %collective-permute-done.6 = bf16[128,9,212]{0,2,1:T(8,128)(2,1)S(1)} collective-permute-done((bf16[128,9,212]{0,2,1:T(8,128)(2,1)S(1)}, bf16[128,9,212]{0,2,1:T(8,128)(2,1)S(1)}, u32[]{:S(2)}, u32[]{:S(2)}) %collective-permute-start.6) | collective-permute-done | bytes 488480 | tf_op jit(solution)/shard_map/ppermute | solution.py:19
  93.7 3.2 %copy-done = bf16[2048,9,212]{0,2,1:T(8,128)(2,1)} copy-done((bf16[2048,9,212]{0,2,1:T(8,128)(2,1)}, bf16[2048,9,212]{0,2,1:T(8,128)(2,1)S(1)}, u32[]{:S(2)}) %copy-start) | copy-done | bytes 7815192
  96.9 2.6 constant_dynamic-slice_fusion.16
  99.5 5.5 %reshape.110 = bf16[1024,1908]{0,1:T(8,128)(2,1)} reshape(bf16[1024,9,212]{0,2,1:T(8,128)(2,1)} %constant_dynamic-slice_fusion.16) | data formatting | bytes 7815168 | tf_op jit(solution)/shard_map/reshape | solution.py:138
  105.1 5.1 %fusion.114 = f32[1024,512]{0,1:T(8,128)S(1)} fusion(bf16[1024,1908]{0,1:T(8,128)(2,1)} %reshape.110, bf16[1908,512]{1,0:T(8,128)(2,1)} %bitcast.281), kind=kOutput, calls=%fused_computation.258 | convolution fusion | flops 2000683008 | bytes 7958528 | tf_op jit(solution)/shard_map/dot_general | solution.py:139
  126.7 2.4 copy.10
  199.9 2.3 collective-permute-start.31
  202.3 2.6 collective-permute-done.31
  204.9 2.3 collective-permute-start.32
  212.7 3.1 %fusion.35 = bf16[512,512]{0,1:T(8,128)(2,1)S(1)} fusion(f32[512,512]{0,1:T(8,128)} %get-tuple-element.63, f32[512,4,128]{0,2,1:T(8,128)S(1)} %copy-done.6, f32[512,512]{0,1:T(8,128)S(1)} %get-tuple-element.41, bf16[512,512]{0,1:T(8,128)(2,1)} %collective-permute-done.12, bf16[512,512]{0,1:T(8,128)(2,1)} %get-tuple-element.35, pred[]{:T(512)S(6)} %eq.32, ...), kind=kOutput, calls=%fused_computation.56 | convolution fusion | flops 547618816 | bytes 5767169 | tf_op jit(solution)/shard_map/dot_general | solution.py:159
  218.1 3.8 %collective-permute-done.34 = f32[32,1024]{1,0:T(8,128)S(1)} collective-permute-done((f32[32,1024]{1,0:T(8,128)S(1)}, f32[32,1024]{1,0:T(8,128)S(1)}, u32[]{:S(2)}, u32[]{:S(2)}) %collective-permute-start.34) | collective-permute-done | bytes 131104 | tf_op jit(solution)/shard_map/ppermute | solution.py:109
  224.1 2.9 %collective-permute-done.35 = f32[32,1024]{1,0:T(8,128)S(1)} collective-permute-done((f32[32,1024]{1,0:T(8,128)S(1)}, f32[32,1024]{1,0:T(8,128)S(1)}, u32[]{:S(2)}, u32[]{:S(2)}) %collective-permute-start.35) | collective-permute-done | bytes 131104 | tf_op jit(solution)/shard_map/ppermute | solution.py:109
  229.4 2.6 collective-permute-done.36
  236.1 4.6 %collective-permute-start.14 = (bf16[1024,1,128]{0,2,1:T(8,128)(2,1)S(1)}, bf16[1024,1,128]{0,2,1:T(8,128)(2,1)S(1)}, u32[]{:S(2)}, u32[]{:S(2)}) collective-permute-start(bf16[1024,1,128]{0,2,1:T(8,128)(2,1)S(1)} %get-tuple-element.53), channel_id=1, source_target_pairs={{0,2},{2,4},{4,6},{6,8},{8,10},{10,12},{12,14},{1,3},{3,5},{5,7},{... | collective-permute-start | bytes 786440 | tf_op jit(solution)/shard_map/ppermute | solution.py:31
  243.4 3.3 %collective-permute-done.38 = f32[32,1024]{1,0:T(8,128)S(1)} collective-permute-done((f32[32,1024]{1,0:T(8,128)S(1)}, f32[32,1024]{1,0:T(8,128)S(1)}, u32[]{:S(2)}, u32[]{:S(2)}) %collective-permute-start.38) | collective-permute-done | bytes 131104 | tf_op jit(solution)/shard_map/ppermute | solution.py:114
  246.7 2.5 collective-permute-start.39
  251.0 2.5 collective-permute-start.25
  262.6 2.8 collective-permute-done.40
  267.5 3.3 %collective-permute-done.41 = f32[32,1024]{1,0:T(8,128)S(1)} collective-permute-done((f32[32,1024]{1,0:T(8,128)S(1)}, f32[32,1024]{1,0:T(8,128)S(1)}, u32[]{:S(2)}, u32[]{:S(2)}) %collective-permute-start.41) | collective-permute-done | bytes 131104 | tf_op jit(solution)/shard_map/ppermute | solution.py:114
  272.9 4.1 %collective-permute-done.42 = f32[32,1024]{1,0:T(8,128)S(1)} collective-permute-done((f32[32,1024]{1,0:T(8,128)S(1)}, f32[32,1024]{1,0:T(8,128)S(1)}, u32[]{:S(2)}, u32[]{:S(2)}) %collective-permute-start.42) | collective-permute-done | bytes 131104 | tf_op jit(solution)/shard_map/ppermute | solution.py:114
  279.1 2.8 collective-permute-done.43
  (306 shorter events, 128.4 us)
Async XLA Ops:
  0.6 31.2 %collective-permute-start = (bf16[128,9,212]{0,2,1:T(8,128)(2,1)}, bf16[128,9,212]{0,2,1:T(8,128)(2,1)S(1)}, u32[]{:S(2)}, u32[]{:S(2)}) collective-permute-start(bf16[128,9,212]{0,2,1:T(8,128)(2,1)} %param.15), channel_id=1, source_target_pairs={{0,2},{2,4},{4,6},{6,8},{8,10},{10,12},{12,14},{14,0},{1,3},{3,5},... | collective-permute-start | bytes 1465352 | tf_op jit(solution)/shard_map/ppermute | solution.py:17
  4.9 15.8 %collective-permute-start.8 = (bf16[212,1,128]{2,1,0:T(2,128)(2,1)S(1)}, bf16[212,1,128]{2,1,0:T(2,128)(2,1)S(1)}, u32[]{:S(2)}, u32[]{:S(2)}) collective-permute-start(bf16[212,1,128]{2,1,0:T(2,128)(2,1)S(1)} %get-tuple-element.60), channel_id=1, source_target_pairs={{2,0},{4,2},{6,4},{8,6},{10,8},{12,10},{14,12},{3,1},{5,3},{7,5},{... | collective-permute-start | bytes 162824 | tf_op jit(solution)/shard_map/ppermute | solution.py:32
  6.2 23.6 %collective-permute-start.7 = (bf16[212,1,128]{2,1,0:T(2,128)(2,1)S(1)}, bf16[212,1,128]{2,1,0:T(2,128)(2,1)S(1)}, u32[]{:S(2)}, u32[]{:S(2)}) collective-permute-start(bf16[212,1,128]{2,1,0:T(2,128)(2,1)S(1)} %get-tuple-element.59), channel_id=1, source_target_pairs={{0,2},{2,4},{4,6},{6,8},{8,10},{10,12},{12,14},{1,3},{3,5},{5,7},{... | collective-permute-start | bytes 162824 | tf_op jit(solution)/shard_map/ppermute | solution.py:31
  10.8 36.7 %collective-permute-start.4 = (bf16[128,9,212]{0,2,1:T(8,128)(2,1)}, bf16[128,9,212]{0,2,1:T(8,128)(2,1)S(1)}, u32[]{:S(2)}, u32[]{:S(2)}) collective-permute-start(bf16[128,9,212]{0,2,1:T(8,128)(2,1)} %param.15), channel_id=1, source_target_pairs={{0,14},{2,0},{4,2},{6,4},{8,6},{10,8},{12,10},{14,12},{1,15},{3,1}... | collective-permute-start | bytes 1465352 | tf_op jit(solution)/shard_map/ppermute | solution.py:19
  31.9 15.0 %collective-permute-start.1 = (bf16[128,9,212]{0,2,1:T(8,128)(2,1)S(1)}, bf16[128,9,212]{0,2,1:T(8,128)(2,1)S(1)}, u32[]{:S(2)}, u32[]{:S(2)}) collective-permute-start(bf16[128,9,212]{0,2,1:T(8,128)(2,1)S(1)} %collective-permute-done), channel_id=1, source_target_pairs={{0,2},{2,4},{4,6},{6,8},{8,10},{10,12},{12,14},{14,0},{1,3},{3,5},... | collective-permute-start | bytes 1465352 | tf_op jit(solution)/shard_map/ppermute | solution.py:17
  46.9 19.8 %collective-permute-start.2 = (bf16[128,9,212]{0,2,1:T(8,128)(2,1)S(1)}, bf16[128,9,212]{0,2,1:T(8,128)(2,1)S(1)}, u32[]{:S(2)}, u32[]{:S(2)}) collective-permute-start(bf16[128,9,212]{0,2,1:T(8,128)(2,1)S(1)} %collective-permute-done.1), channel_id=1, source_target_pairs={{0,2},{2,4},{4,6},{6,8},{8,10},{10,12},{12,14},{14,0},{1,3},{3,5},... | collective-permute-start | bytes 1465352 | tf_op jit(solution)/shard_map/ppermute | solution.py:17
  47.5 25.0 %collective-permute-start.5 = (bf16[128,9,212]{0,2,1:T(8,128)(2,1)S(1)}, bf16[128,9,212]{0,2,1:T(8,128)(2,1)S(1)}, u32[]{:S(2)}, u32[]{:S(2)}) collective-permute-start(bf16[128,9,212]{0,2,1:T(8,128)(2,1)S(1)} %collective-permute-done.4), channel_id=1, source_target_pairs={{0,14},{2,0},{4,2},{6,4},{8,6},{10,8},{12,10},{14,12},{1,15},{3,1}... | collective-permute-start | bytes 1465352 | tf_op jit(solution)/shard_map/ppermute | solution.py:19
  66.7 14.6 %collective-permute-start.3 = (bf16[128,9,212]{0,2,1:T(8,128)(2,1)S(1)}, bf16[128,9,212]{0,2,1:T(8,128)(2,1)S(1)}, u32[]{:S(2)}, u32[]{:S(2)}) collective-permute-start(bf16[128,9,212]{0,2,1:T(8,128)(2,1)S(1)} %collective-permute-done.2), channel_id=1, source_target_pairs={{0,2},{2,4},{4,6},{6,8},{8,10},{10,12},{12,14},{14,0},{1,3},{3,5},... | collective-permute-start | bytes 1465352 | tf_op jit(solution)/shard_map/ppermute | solution.py:17
  72.4 19.6 %collective-permute-start.6 = (bf16[128,9,212]{0,2,1:T(8,128)(2,1)S(1)}, bf16[128,9,212]{0,2,1:T(8,128)(2,1)S(1)}, u32[]{:S(2)}, u32[]{:S(2)}) collective-permute-start(bf16[128,9,212]{0,2,1:T(8,128)(2,1)S(1)} %collective-permute-done.5), channel_id=1, source_target_pairs={{0,14},{2,0},{4,2},{6,4},{8,6},{10,8},{12,10},{14,12},{1,15},{3,1}... | collective-permute-start | bytes 1465352 | tf_op jit(solution)/shard_map/ppermute | solution.py:19
  111.4 18.4 %collective-permute-start.9 = (f32[512,512]{0,1:T(8,128)}, f32[512,512]{0,1:T(8,128)}, u32[]{:S(2)}, u32[]{:S(2)}) collective-permute-start(f32[512,512]{0,1:T(8,128)} %slice_select_fusion), channel_id=1, source_target_pairs={{0,1},{1,0},{2,3},{3,2},{4,5},{5,4},{6,7},{7,6},{8,9},{9,8},{10,11... | collective-permute-start | bytes 3145736 | tf_op jit(solution)/shard_map/ppermute | solution.py:65
  115.1 97.6 %collective-permute-start.11 = (bf16[512,512]{0,1:T(8,128)(2,1)}, bf16[512,512]{0,1:T(8,128)(2,1)}, u32[]{:S(2)}, u32[]{:S(2)}) collective-permute-start(bf16[512,512]{0,1:T(8,128)(2,1)} %get-tuple-element.56), channel_id=1, source_target_pairs={{0,1},{1,0},{2,3},{3,2},{4,5},{5,4},{6,7},{7,6},{8,9},{9,8},{10,11... | collective-permute-start | bytes 1572872 | tf_op jit(solution)/shard_map/ppermute | solution.py:152
  138.2 74.5 %collective-permute-start.12 = (bf16[512,512]{0,1:T(8,128)(2,1)}, bf16[512,512]{0,1:T(8,128)(2,1)}, u32[]{:S(2)}, u32[]{:S(2)}) collective-permute-start(bf16[512,512]{0,1:T(8,128)(2,1)} %get-tuple-element.35), channel_id=1, source_target_pairs={{0,1},{1,0},{2,3},{3,2},{4,5},{5,4},{6,7},{7,6},{8,9},{9,8},{10,11... | collective-permute-start | bytes 1572872 | tf_op jit(solution)/shard_map/ppermute | solution.py:54
  140.9 59.0 %collective-permute-start.30 = (f32[32,1024]{1,0:T(8,128)S(1)}, f32[32,1024]{1,0:T(8,128)S(1)}, u32[]{:S(2)}, u32[]{:S(2)}) collective-permute-start(f32[32,1024]{1,0:T(8,128)S(1)} %select_bitcast_fusion), channel_id=1, source_target_pairs={{2,0},{6,2},{10,6},{14,10},{12,14},{8,12},{4,8},{0,4},{3,1},{7,3},... | collective-permute-start | bytes 393224 | tf_op jit(solution)/shard_map/ppermute | solution.py:109
  191.3 10.9 %collective-permute-start.16 = (f32[32,1024]{1,0:T(8,128)}, f32[32,1024]{1,0:T(8,128)S(1)}, u32[]{:S(2)}, u32[]{:S(2)}) collective-permute-start(f32[32,1024]{1,0:T(8,128)} %select_bitcast_fusion.1), channel_id=1, source_target_pairs={{0,2},{2,6},{6,10},{10,14},{14,12},{12,8},{8,4},{4,0},{1,3},{3,7},... | collective-permute-start | bytes 393224 | tf_op jit(solution)/shard_map/ppermute | solution.py:109
  210.0 6.0 %collective-permute-start.33 = (f32[32,1024]{1,0:T(8,128)S(1)}, f32[32,1024]{1,0:T(8,128)S(1)}, u32[]{:S(2)}, u32[]{:S(2)}) collective-permute-start(f32[32,1024]{1,0:T(8,128)S(1)} %bitcast_add_fusion.4), channel_id=1, source_target_pairs={{2,0},{6,2},{10,6},{14,10},{12,14},{8,12},{4,8},{0,4},{3,1},{7,3},... | collective-permute-start | bytes 393224 | tf_op jit(solution)/shard_map/ppermute | solution.py:109
  212.6 5.5 %collective-permute-start.19 = (f32[32,1024]{1,0:T(8,128)S(1)}, f32[32,1024]{1,0:T(8,128)S(1)}, u32[]{:S(2)}, u32[]{:S(2)}) collective-permute-start(f32[32,1024]{1,0:T(8,128)S(1)} %bitcast_add_fusion.11), channel_id=1, source_target_pairs={{0,2},{2,6},{6,10},{10,14},{14,12},{12,8},{8,4},{4,0},{1,3},{3,7},... | collective-permute-start | bytes 393224 | tf_op jit(solution)/shard_map/ppermute | solution.py:109
  215.9 18.6 %collective-permute-start.13 = (bf16[512,4,128]{0,2,1:T(8,128)(2,1)S(1)}, bf16[512,4,128]{0,2,1:T(8,128)(2,1)S(1)}, u32[]{:S(2)}, u32[]{:S(2)}) collective-permute-start(bf16[512,4,128]{0,2,1:T(8,128)(2,1)S(1)} %bitcast.282), channel_id=1, source_target_pairs={{0,1},{1,0},{2,3},{3,2},{4,5},{5,4},{6,7},{7,6},{8,9},{9,8},{10,11... | collective-permute-start | bytes 1572872 | tf_op jit(solution)/shard_map/ppermute | solution.py:54
  216.0 5.9 %collective-permute-start.34 = (f32[32,1024]{1,0:T(8,128)S(1)}, f32[32,1024]{1,0:T(8,128)S(1)}, u32[]{:S(2)}, u32[]{:S(2)}) collective-permute-start(f32[32,1024]{1,0:T(8,128)S(1)} %bitcast_add_fusion.3), channel_id=1, source_target_pairs={{2,0},{6,2},{10,6},{14,10},{12,14},{8,12},{4,8},{0,4},{3,1},{7,3},... | collective-permute-start | bytes 393224 | tf_op jit(solution)/shard_map/ppermute | solution.py:109
  218.1 5.9 %collective-permute-start.20 = (f32[32,1024]{1,0:T(8,128)S(1)}, f32[32,1024]{1,0:T(8,128)S(1)}, u32[]{:S(2)}, u32[]{:S(2)}) collective-permute-start(f32[32,1024]{1,0:T(8,128)S(1)} %bitcast_add_fusion.10), channel_id=1, source_target_pairs={{0,2},{2,6},{6,10},{10,14},{14,12},{12,8},{8,4},{4,0},{1,3},{3,7},... | collective-permute-start | bytes 393224 | tf_op jit(solution)/shard_map/ppermute | solution.py:109
  232.1 9.2 %collective-permute-start.37 = (f32[32,1024]{1,0:T(8,128)S(1)}, f32[32,1024]{1,0:T(8,128)S(1)}, u32[]{:S(2)}, u32[]{:S(2)}) collective-permute-start(f32[32,1024]{1,0:T(8,128)S(1)} %get-tuple-element.39), channel_id=1, source_target_pairs={{2,0},{6,2},{10,6},{14,10},{12,14},{8,12},{4,8},{0,4},{3,1},{7,3},... | collective-permute-start | bytes 393224 | tf_op jit(solution)/shard_map/ppermute | solution.py:114
  234.2 8.9 %collective-permute-start.23 = (f32[32,1024]{1,0:T(8,128)S(1)}, f32[32,1024]{1,0:T(8,128)S(1)}, u32[]{:S(2)}, u32[]{:S(2)}) collective-permute-start(f32[32,1024]{1,0:T(8,128)S(1)} %get-tuple-element.37), channel_id=1, source_target_pairs={{0,2},{2,6},{6,10},{10,14},{14,12},{12,8},{8,4},{4,0},{1,3},{3,7},... | collective-permute-start | bytes 393224 | tf_op jit(solution)/shard_map/ppermute | solution.py:114
  234.8 18.7 %collective-permute-start.15 = (bf16[1024,1,128]{0,2,1:T(8,128)(2,1)S(1)}, bf16[1024,1,128]{0,2,1:T(8,128)(2,1)S(1)}, u32[]{:S(2)}, u32[]{:S(2)}) collective-permute-start(bf16[1024,1,128]{0,2,1:T(8,128)(2,1)S(1)} %get-tuple-element.54), channel_id=1, source_target_pairs={{2,0},{4,2},{6,4},{8,6},{10,8},{12,10},{14,12},{3,1},{5,3},{7,5},{... | collective-permute-start | bytes 786440 | tf_op jit(solution)/shard_map/ppermute | solution.py:32
  236.1 17.4 %collective-permute-start.14 = (bf16[1024,1,128]{0,2,1:T(8,128)(2,1)S(1)}, bf16[1024,1,128]{0,2,1:T(8,128)(2,1)S(1)}, u32[]{:S(2)}, u32[]{:S(2)}) collective-permute-start(bf16[1024,1,128]{0,2,1:T(8,128)(2,1)S(1)} %get-tuple-element.53), channel_id=1, source_target_pairs={{0,2},{2,4},{4,6},{6,8},{8,10},{10,12},{12,14},{1,3},{3,5},{5,7},{... | collective-permute-start | bytes 786440 | tf_op jit(solution)/shard_map/ppermute | solution.py:31
  241.3 5.4 %collective-permute-start.38 = (f32[32,1024]{1,0:T(8,128)S(1)}, f32[32,1024]{1,0:T(8,128)S(1)}, u32[]{:S(2)}, u32[]{:S(2)}) collective-permute-start(f32[32,1024]{1,0:T(8,128)S(1)} %collective-permute-done.37), channel_id=1, source_target_pairs={{2,0},{6,2},{10,6},{14,10},{12,14},{8,12},{4,8},{0,4},{3,1},{7,3},... | collective-permute-start | bytes 393224 | tf_op jit(solution)/shard_map/ppermute | solution.py:114
  243.1 7.9 %collective-permute-start.24 = (f32[32,1024]{1,0:T(8,128)S(1)}, f32[32,1024]{1,0:T(8,128)S(1)}, u32[]{:S(2)}, u32[]{:S(2)}) collective-permute-start(f32[32,1024]{1,0:T(8,128)S(1)} %collective-permute-done.23), channel_id=1, source_target_pairs={{0,2},{2,6},{6,10},{10,14},{14,12},{12,8},{8,4},{4,0},{1,3},{3,7},... | collective-permute-start | bytes 393224 | tf_op jit(solution)/shard_map/ppermute | solution.py:114
  246.7 13.8 %collective-permute-start.39 = (f32[32,1024]{1,0:T(8,128)S(1)}, f32[32,1024]{1,0:T(8,128)S(1)}, u32[]{:S(2)}, u32[]{:S(2)}) collective-permute-start(f32[32,1024]{1,0:T(8,128)S(1)} %collective-permute-done.38), channel_id=1, source_target_pairs={{2,0},{6,2},{10,6},{14,10},{12,14},{8,12},{4,8},{0,4},{3,1},{7,3},... | collective-permute-start | bytes 393224 | tf_op jit(solution)/shard_map/ppermute | solution.py:114
  251.0 9.5 %collective-permute-start.25 = (f32[32,1024]{1,0:T(8,128)S(1)}, f32[32,1024]{1,0:T(8,128)S(1)}, u32[]{:S(2)}, u32[]{:S(2)}) collective-permute-start(f32[32,1024]{1,0:T(8,128)S(1)} %collective-permute-done.24), channel_id=1, source_target_pairs={{0,2},{2,6},{6,10},{10,14},{14,12},{12,8},{8,4},{4,0},{1,3},{3,7},... | collective-permute-start | bytes 393224 | tf_op jit(solution)/shard_map/ppermute | solution.py:114
  265.4 5.4 %collective-permute-start.41 = (f32[32,1024]{1,0:T(8,128)S(1)}, f32[32,1024]{1,0:T(8,128)S(1)}, u32[]{:S(2)}, u32[]{:S(2)}) collective-permute-start(f32[32,1024]{1,0:T(8,128)S(1)} %collective-permute-done.40), channel_id=1, source_target_pairs={{2,0},{6,2},{10,6},{14,10},{12,14},{8,12},{4,8},{0,4},{3,1},{7,3},... | collective-permute-start | bytes 393224 | tf_op jit(solution)/shard_map/ppermute | solution.py:114
  265.5 5.4 %collective-permute-start.27 = (f32[32,1024]{1,0:T(8,128)S(1)}, f32[32,1024]{1,0:T(8,128)S(1)}, u32[]{:S(2)}, u32[]{:S(2)}) collective-permute-start(f32[32,1024]{1,0:T(8,128)S(1)} %collective-permute-done.26), channel_id=1, source_target_pairs={{0,2},{2,6},{6,10},{10,14},{14,12},{12,8},{8,4},{4,0},{1,3},{3,7},... | collective-permute-start | bytes 393224 | tf_op jit(solution)/shard_map/ppermute | solution.py:114
  270.8 6.2 %collective-permute-start.42 = (f32[32,1024]{1,0:T(8,128)S(1)}, f32[32,1024]{1,0:T(8,128)S(1)}, u32[]{:S(2)}, u32[]{:S(2)}) collective-permute-start(f32[32,1024]{1,0:T(8,128)S(1)} %collective-permute-done.41), channel_id=1, source_target_pairs={{2,0},{6,2},{10,6},{14,10},{12,14},{8,12},{4,8},{0,4},{3,1},{7,3},... | collective-permute-start | bytes 393224 | tf_op jit(solution)/shard_map/ppermute | solution.py:114
  270.9 6.3 %collective-permute-start.28 = (f32[32,1024]{1,0:T(8,128)S(1)}, f32[32,1024]{1,0:T(8,128)S(1)}, u32[]{:S(2)}, u32[]{:S(2)}) collective-permute-start(f32[32,1024]{1,0:T(8,128)S(1)} %collective-permute-done.27), channel_id=1, source_target_pairs={{0,2},{2,6},{6,10},{10,14},{14,12},{12,8},{8,4},{4,0},{1,3},{3,7},... | collective-permute-start | bytes 393224 | tf_op jit(solution)/shard_map/ppermute | solution.py:114
  277.2 5.8 %collective-permute-start.29 = (f32[32,1024]{1,0:T(8,128)S(1)}, f32[32,1024]{1,0:T(8,128)S(1)}, u32[]{:S(2)}, u32[]{:S(2)}) collective-permute-start(f32[32,1024]{1,0:T(8,128)S(1)} %collective-permute-done.28), channel_id=1, source_target_pairs={{0,2},{2,6},{6,10},{10,14},{14,12},{12,8},{8,4},{4,0},{1,3},{3,7},... | collective-permute-start | bytes 393224 | tf_op jit(solution)/shard_map/ppermute | solution.py:114
  (72 other events, 599.2 us)
